TPU v7x, 32 devices: a whole 2x2x4 slice. The times are simulated.
32 devices in a mesh: grp: 2 (over x), tile: 16 (over z, y, core).
Axes of the slice: x: 2, y: 2, z: 4, core: 2. Of those that a mesh axis runs over, the one named last changes fastest.
Arguments:
- latents: bfloat16 [384, 16, 8, 256], P(('grp', 'tile')), parts along dimension 0, may hold values from -6 to 6
- frame_counts: int32 [32], P('grp'), parts along dimension 0, may hold values from 1 to 12, 64 in all
- clip_order: int32 [32], P('grp'), parts along dimension 0, may hold values from 0 to 15, each once
- norm_scale: float32 [256], replicated, may hold values from 0.25 to 1.75
- norm_offset: float32 [256], replicated, may hold values from -3 to 3
- conv_weight: bfloat16 [3, 3, 3, 256, 256], replicated, may hold values from -0.078125 to 0.078125
- conv_bias: float32 [256], replicated, may hold values from -3 to 3
- out_scale: float32 [256], replicated, may hold values from 0.25 to 1.75
- out_offset: float32 [256], replicated, may hold values from -3 to 3
Outputs:
- block_out: bfloat16 [2, 1024, 8, 256], P(None, ('grp', 'tile')), parts along dimension 1
- normed: bfloat16 [2, 1024, 8, 256], P(None, ('grp', 'tile')), parts along dimension 1
There are 2 independent parts, one for each index of `grp`. A program takes and returns all parts, laid end to end along the dimension named above; an argument that names none is the same for every part. Nothing has to cross between parts.
Inputs may be any that keep to these rules, and one draw needn't show every extreme that they name: `frame_counts`: they sum to 64; the largest is exactly 12. `clip_order`: A permutation of the clips.
All inputs are finite; a program needn't handle non-finite values.
Results may differ from a plain program's by a relative error of at most 0.0057.
Values may be sent and summed in bfloat16 or wider, within the bound.
No kernel may reach another device: no remote copies, remote signals or barrier semaphores. Data moves between devices by JAX's collectives and lax.ppermute only.
A program may use at most 64 MiB of HBM per device.

v0:
```python
import jax
import jax.numpy as jnp
from jax import lax
from jax.sharding import PartitionSpec as P

GROUPS = 32
MEANF = 4
NRB = 8
eps = 1e-06


def normalize(values, frame_count, scaling, offsets):
    frames = values.shape[0]
    channels = values.shape[-1]
    grouped = values.reshape(frames, -1, GROUPS, channels // GROUPS)
    live_mask = (jnp.arange(frames) < frame_count).astype(jnp.float32)[:, None, None, None]
    members = frame_count.astype(jnp.float32) * grouped.shape[1] * grouped.shape[3]
    group_mean = jnp.sum(grouped * live_mask, axis=(0, 1, 3)) / members
    spread = (
        jnp.sum(grouped * grouped * live_mask, axis=(0, 1, 3)) / members - group_mean * group_mean
    )
    inverse = lax.rsqrt(spread + eps)
    normed = (grouped - group_mean[:, None]) * inverse[:, None] * scaling.reshape(
        GROUPS, -1
    ) + offsets.reshape(GROUPS, -1)
    return jax.nn.silu(normed).reshape(values.shape)


def convolve(stacked, kernel, offsets):
    tile_rows = stacked.shape[1] - 2
    columns = stacked.shape[3]
    channels = stacked.shape[4]
    padded = jnp.pad(stacked, ((0, 0), (0, 0), (0, 0), (1, 1), (0, 0)))
    tap_list = [
        padded[frame_lag, row_tap : row_tap + tile_rows, :, col_tap : col_tap + columns]
        for frame_lag in range(3)
        for row_tap in range(3)
        for col_tap in range(3)
    ]
    unfolded = jnp.concatenate(tap_list, axis=-1)
    result = jnp.dot(
        unfolded.reshape(-1, 27 * channels),
        kernel.reshape(27 * channels, -1),
        preferred_element_type=jnp.float32,
    )
    return (result + offsets).reshape(tile_rows, stacked.shape[2], columns, -1)


def local(
    latents,
    frame_counts,
    clip_order,
    norm_scale,
    norm_offset,
    conv_weight,
    conv_bias,
    out_scale,
    out_offset,
):
    devices = lax.axis_size("tile")
    device = lax.axis_index("tile")
    frames, frame_rows, columns, channels = latents.shape
    tile_rows = frame_rows // NRB
    own_tiles = frames * NRB
    capacity = (own_tiles + devices - 1) // devices
    slots_all = devices * capacity
    worker_tiles = MEANF * NRB
    positions = jnp.arange(frame_counts.shape[0], dtype=jnp.int32)
    chosen = clip_order[:, None] == positions[None, :]
    ordered = jnp.sum(jnp.where(chosen, frame_counts[None, :], 0), axis=1)
    starts = (jnp.cumsum(ordered) - ordered) * NRB
    own_start = jnp.sum(jnp.where(clip_order == device, starts, 0))
    own_count = jnp.sum(jnp.where(positions == device, frame_counts, 0))
    active = normalize(latents.astype(jnp.float32), own_count, norm_scale, norm_offset).astype(
        jnp.bfloat16
    )
    outgoing_slot = jnp.arange(slots_all, dtype=jnp.int32)
    target = outgoing_slot // capacity
    source_tile = outgoing_slot % capacity * devices + (target - own_start) % devices
    sendable = source_tile < own_count * NRB
    source_tile = jnp.minimum(source_tile, own_tiles - 1)
    local_slot = jnp.arange(worker_tiles, dtype=jnp.int32)
    tile_id = local_slot * devices + device
    placed = jnp.sum((starts[None, :] <= tile_id[:, None]).astype(jnp.int32), axis=1) - 1
    at_place = placed[:, None] == positions[None, :]
    clip_id = jnp.sum(jnp.where(at_place, clip_order[None, :], 0), axis=1)
    within = tile_id - jnp.sum(jnp.where(at_place, starts[None, :], 0), axis=1)
    take_from = clip_id * capacity + within // devices
    padded = jnp.pad(active, ((2, 0), (1, 1), (0, 0), (0, 0)))
    lagged = []
    for frame_lag in range(3):
        window = padded[frame_lag : frame_lag + frames]
        row_bands = [
            window[:, row_start : row_start + NRB * tile_rows : tile_rows]
            for row_start in range(tile_rows + 2)
        ]
        lagged.append(jnp.stack(row_bands, 0))
    pieces = jnp.stack(lagged, 0).reshape(3, tile_rows + 2, own_tiles, columns, channels)
    outgoing = jnp.where(
        sendable[None, None, :, None, None], jnp.take(pieces, source_tile, axis=2), 0
    )
    received = lax.all_to_all(outgoing, "tile", split_axis=2, concat_axis=2, tiled=True)
    stacked = jnp.take(received, take_from, axis=2)
    block_out = convolve(stacked, conv_weight, conv_bias).astype(jnp.bfloat16)
    per_group = channels // GROUPS
    grouped = block_out.astype(jnp.float32).reshape(
        tile_rows, worker_tiles, columns, GROUPS, per_group
    )
    first_sum = jnp.sum(grouped, axis=(0, 2, 4))
    second_sum = jnp.sum(grouped * grouped, axis=(0, 2, 4))
    belongs = (clip_id[:, None] == positions[None, :]).astype(jnp.float32)
    totals = lax.psum(
        (
            jnp.dot(belongs.T, first_sum, precision=lax.Precision.HIGHEST),
            jnp.dot(belongs.T, second_sum, precision=lax.Precision.HIGHEST),
        ),
        "tile",
    )
    members = frame_counts.astype(jnp.float32) * (frame_rows * columns * per_group)
    clip_mean = totals[0] / members[:, None]
    clip_spread = totals[1] / members[:, None] - clip_mean * clip_mean
    clip_inverse = lax.rsqrt(clip_spread + eps)
    tile_mean = jnp.dot(belongs, clip_mean, precision=lax.Precision.HIGHEST)
    tile_inverse = jnp.dot(belongs, clip_inverse, precision=lax.Precision.HIGHEST)
    normed = (grouped - tile_mean[None, :, None, :, None]) * tile_inverse[
        None, :, None, :, None
    ] * out_scale.reshape(GROUPS, per_group) + out_offset.reshape(GROUPS, per_group)
    normed = jax.nn.silu(normed).astype(jnp.bfloat16).reshape(block_out.shape)
    return (block_out, normed)


def solution(mesh):
    in_specs = (
        P(("grp", "tile"), None, None, None),
        P("grp"),
        P("grp"),
        P(),
        P(),
        P(),
        P(),
        P(),
        P(),
    )
    out_specs = (P(None, ("grp", "tile"), None, None), P(None, ("grp", "tile"), None, None))
    return jax.shard_map(local, mesh=mesh, in_specs=in_specs, out_specs=out_specs, check_vma=False)
```

profile of v0, /device:TPU:0, one launch (start us, length us, event | category | flops | bytes accessed | tf_op | source)
XLA Modules:
  0.0 250.5 jit_solution(12813425869111469504)
XLA Ops:
  2.4 2.0 fusion.32
  5.5 1.2 fusion.39
  6.7 1.3 compare_and_fusion
  8.0 2.2 fusion.11
  11.0 1.4 reduce_sum.116
  17.1 1.7 fusion.9
  19.1 1.3 fusion.44
  20.3 1.2 fusion.46
  24.0 5.2 %maximum_maximum_fusion = bf16[3,4,96,8,256]{4,3,2,1,0:T(8,128)(2,1)} fusion(bf16[1,1,96,8,256]{4,3,2,1,0:T(8,128)(2,1)} %bitcast.72, bf16[1,1,96,8,256]{4,3,2,1,0:T(8,128)(2,1)} %bitcast.73, bf16[1,1,96,8,256]{4,3,2,1,0:T(8,128)(2,1)} %bitcast.74, bf16[1,1,96,8,256]{4,3,2,1,0:T(8,128)(2,1)} %bitcast.71, bf16[1,1,96,8,256]{4,3,2,1,0:T(8,128)(2,1)} %bitcast.76, ...), kind=kLoop, calls=%fused_computation.21 | loop fusion | flops 25952256 | bytes 9437184 | tf_op jit(solution)/shard_map/stack | solution.py:98
  29.2 5.9 %gather_fusion = bf16[96,3,4,8,256]{4,3,2,1,0:T(8,128)(2,1)} fusion(bf16[3,4,96,8,256]{4,3,2,1,0:T(8,128)(2,1)} %maximum_maximum_fusion, s32[1024]{0:T(1024)S(1)} %pad_clamp_fusion.1), kind=kCustom, calls=%fused_computation | custom fusion | bytes 9437568 | tf_op jit(solution)/shard_map/jit(_take)/gather | solution.py:100
  35.1 5.1 %select_bitcast_fusion = bf16[3,4,96,8,256]{4,3,1,0,2:T(8,128)(2,1)} fusion(bf16[96,3,4,8,256]{4,3,2,1,0:T(8,128)(2,1)} %gather_fusion, pred[96]{0:T(512)(128)(4,1)S(1)} %broadcast_compare_fusion, pred[96]{0:T(512)(128)(4,1)S(1)} %copy-done.5), kind=kLoop, calls=%fused_computation.22 | loop fusion | flops 4718592 | bytes 9437376 | tf_op jit(solution)/shard_map/jit(_where)/select_n | solution.py:99
  40.2 7.6 %all-to-all-start = ((bf16[3,4,96,8,256]{4,3,1,0,2:T(8,128)(2,1)}), bf16[3,4,96,8,256]{4,3,1,0,2:T(8,128)(2,1)}, u32[]{:S(2)}, u32[]{:S(2)}) async-start(bf16[3,4,96,8,256]{4,3,1,0,2:T(8,128)(2,1)} %select_bitcast_fusion), calls=%async_computation | async-start | bytes 9437184 | tf_op jit(solution)/shard_map/all_to_all | solution.py:102
  48.1 1.2 convert_multiply_fusion.2
  49.3 85.3 %all-to-all-done = bf16[3,4,96,8,256]{4,3,1,0,2:T(8,128)(2,1)} async-done(((bf16[3,4,96,8,256]{4,3,1,0,2:T(8,128)(2,1)}), bf16[3,4,96,8,256]{4,3,1,0,2:T(8,128)(2,1)}, u32[]{:S(2)}, u32[]{:S(2)}) %all-to-all-start) | async-done | bytes 4718624 | tf_op jit(solution)/shard_map/all_to_all | solution.py:102
  134.6 4.9 %copy.83 = bf16[3,4,96,8,256]{4,3,2,1,0:T(8,128)(2,1)} copy(bf16[3,4,96,8,256]{4,3,1,0,2:T(8,128)(2,1)} %all-to-all-done) | data formatting | bytes 9437184 | tf_op jit(solution)/shard_map/all_to_all | solution.py:102
  139.5 4.2 %gather_fusion.1 = bf16[32,3,4,8,256]{4,3,2,1,0:T(8,128)(2,1)} fusion(bf16[3,4,96,8,256]{4,3,2,1,0:T(8,128)(2,1)} %copy.83, s32[1024]{0:T(1024)S(1)} %pad_clamp_fusion), kind=kCustom, calls=%fused_computation.1 | custom fusion | bytes 3145856 | tf_op jit(solution)/shard_map/jit(_take)/gather | solution.py:103
  143.8 1.6 select_bitcast_fusion.1
  148.5 2.7 %fusion.12 = bf16[512,256]{1,0:T(8,128)(2,1)} fusion(bf16[512,6912]{1,0:T(8,128)(2,1)S(1)} %constant_dynamic-update-slice_fusion, bf16[6912,256]{1,0:T(8,128)(2,1)S(1)} %bitcast.66, f32[256]{0:T(256)S(1)} %copy-done.7), kind=kOutput, calls=%fused_computation.40 | convolution fusion | flops 1812201472 | bytes 10880000 | tf_op jit(solution)/shard_map/dot_general | solution.py:41
  151.2 7.0 %reshape.406 = f32[2,32,8,32,8]{4,3,2,1,0:T(8,128)} reshape(bf16[512,256]{1,0:T(8,128)(2,1)} %fusion.12) | data formatting | bytes 786432 | tf_op jit(solution)/shard_map/convert_element_type | solution.py:106
  158.2 5.0 %fusion.42 = (f32[32,32]{1,0:T(8,128)S(1)}, f32[32,32]{1,0:T(8,128)S(1)}) fusion(f32[2,32,8,32,8]{4,3,2,1,0:T(8,128)} %reshape.406), kind=kLoop, calls=%fused_computation.154 | loop fusion | flops 391168 | bytes 532480 | tf_op jit(solution)/shard_map/reduce_sum | solution.py:109
  164.4 77.8 %all-reduce.2 = (f32[16,32]{1,0:T(8,128)}, f32[16,32]{1,0:T(8,128)}) all-reduce(f32[16,32]{1,0:T(8,128)S(1)} %fusion.14, f32[16,32]{1,0:T(8,128)S(1)} %fusion.16), channel_id=1, replica_groups=mesh['grp'=2,'tile'=16] {'tile'}, use_global_device_ids=true, to_apply=%region_14.15 | all-reduce | flops 1024 | bytes 8192 | tf_op jit(solution)/shard_map/psum | solution.py:112
  243.8 1.6 copy.112
  247.1 1.6 copy.114
  248.7 1.9 multiply_convert_fusion
  (102 shorter events, 17.3 us)
Async XLA Ops:
  0.6 147.7 %copy-start = (bf16[3,3,3,256,256]{4,3,2,1,0:T(8,128)(2,1)S(1)}, bf16[3,3,3,256,256]{4,3,2,1,0:T(8,128)(2,1)}, u32[]{:S(2)}) copy-start(bf16[3,3,3,256,256]{4,3,2,1,0:T(8,128)(2,1)} %param.14) | copy-start | bytes 10616836
  1.7 0.5 copy-start.4
  19.1 3.7 %copy-start.6 = (s32[96]{0:T(128)S(1)}, s32[96]{0:T(128)}, u32[]{:S(2)}) copy-start(s32[96]{0:T(128)} %fusion.39) | copy-start | bytes 1156
  29.2 5.9 %copy-start.5 = (pred[96]{0:T(512)(128)(4,1)S(1)}, pred[96]{0:T(512)(128)(4,1)}, u32[]{:S(2)}) copy-start(pred[96]{0:T(512)(128)(4,1)} %compare_and_fusion) | copy-start | bytes 292
  40.2 7.6 %copy-start.3 = (s32[16]{0:T(128)S(1)}, s32[16]{0:T(128)}, u32[]{:S(2)}) copy-start(s32[16]{0:T(128)} %get-tuple-element.11) | copy-start | bytes 196
  40.2 7.7 %copy-start.2 = (s32[16]{0:T(128)S(1)}, s32[16]{0:T(128)}, u32[]{:S(2)}) copy-start(s32[16]{0:T(128)} %param.11) | copy-start | bytes 196
  40.2 94.4 %all-to-all-start = ((bf16[3,4,96,8,256]{4,3,1,0,2:T(8,128)(2,1)}), bf16[3,4,96,8,256]{4,3,1,0,2:T(8,128)(2,1)}, u32[]{:S(2)}, u32[]{:S(2)}) async-start(bf16[3,4,96,8,256]{4,3,1,0,2:T(8,128)(2,1)} %select_bitcast_fusion), calls=%async_computation | async-start | bytes 9437184 | tf_op jit(solution)/shard_map/all_to_all | solution.py:102
  48.0 115.2 %copy-start.1 = (s32[32]{0:T(128)}, s32[32]{0:T(128)S(1)}, u32[]{:S(2)}) copy-start(s32[32]{0:T(128)S(1)} %get-tuple-element.6) | copy-start | bytes 388
  147.8 0.7 copy-start.7
where the time goes:
time: 252 us; the launch traced here: 251 us
  waiting for transfers between devices  85.3 us (34%)
  blocking collectives  77.8 us (31%)
  local copies, waits for them, and re-layouts  37.9 us (15%)
  other arithmetic  33.9 us (13%)
  starting transfers between devices  7.56 us (3%)
  matrix products  5.83 us (2%)
    all_to_all x1, waiting for transfers between devices, local(): lax.all_to_all(outgoing, 'tile', split_axis=2, concat_axis=2, tiled=True)  85.3 us
    psum x1, blocking collectives, local(): lax.psum((jnp.dot(belongs.T, first_sum, precision=lax.Precision.HIGHEST),...  77.8 us
    all_to_all x1, starting transfers between devices, local(): lax.all_to_all(outgoing, 'tile', split_axis=2, concat_axis=2, tiled=True)  7.56 us
    convert_element_type x1, local copies, waits for them, and re-layouts, local(): block_out.astype(jnp.float32)  7 us
    gather x1, local copies, waits for them, and re-layouts, local(): jnp.take(pieces, source_tile, axis=2)  5.85 us
    another operation x1, other arithmetic, local(): jnp.stack(lagged, 0).reshape(3, tile_rows + 2, own_tiles, columns, channels)  5.21 us
    select_n x1, other arithmetic, local(): jnp.where(sendable[None, None, :, None, None], jnp.take(pieces, source_ti...  5.14 us
  transfers between devices with their start and end apart: 1, of which 1 were waited for; matrix products, arithmetic and copies ran while one was open for 1% of the time, Pallas kernels for 0%

commit v1 on v0

--- a/solution.py
+++ b/solution.py
@@ -99,7 +99,10 @@
     outgoing = jnp.where(
         sendable[None, None, :, None, None], jnp.take(pieces, source_tile, axis=2), 0
     )
-    received = lax.all_to_all(outgoing, "tile", split_axis=2, concat_axis=2, tiled=True)
+    received = jnp.concatenate(
+        lax.all_to_all(jnp.stack(jnp.split(outgoing, lax.axis_size("tile"), axis=2)), "tile", 0, 0),
+        axis=2,
+    )
     stacked = jnp.take(received, take_from, axis=2)
     block_out = convolve(stacked, conv_weight, conv_bias).astype(jnp.bfloat16)
     per_group = channels // GROUPS

time: 252 us -> 261 us (1.036)
  local copies, waits for them, and re-layouts: 37.9 us -> 49.7 us
    unnamed x42 -> x57, local copies, waits for them, and re-layouts: 1.22 us -> 12.3 us
    reshape x0 -> x1, local copies, waits for them, and re-layouts: none -> 4.91 us  [local(): jnp.concatenate(lax.all_to_all(jnp.stack(jnp.split(outgoing, lax.axis_siz...]
    all_to_all x1 -> x0, local copies, waits for them, and re-layouts: 4.91 us -> none  [local(): lax.all_to_all(outgoing, 'tile', split_axis=2, concat_axis=2, tiled=True)]
where the time goes in v1:
time: 261 us; the launch traced here: 260 us
  waiting for transfers between devices  85.3 us (33%)
  blocking collectives  77.8 us (30%)
  local copies, waits for them, and re-layouts  49.7 us (19%)
  other arithmetic  31.7 us (12%)
  starting transfers between devices  7.57 us (3%)
  matrix products  5.83 us (2%)
    all_to_all x1, waiting for transfers between devices, local(): lax.all_to_all(jnp.stack(jnp.split(outgoing, lax.axis_size('tile'), axis=...  85.3 us
    psum x1, blocking collectives, local(): lax.psum((jnp.dot(belongs.T, first_sum, precision=lax.Precision.HIGHEST),...  77.8 us
    unnamed x57, local copies, waits for them, and re-layouts  12.3 us
    all_to_all x1, starting transfers between devices, local(): lax.all_to_all(jnp.stack(jnp.split(outgoing, lax.axis_size('tile'), axis=...  7.57 us
    convert_element_type x1, local copies, waits for them, and re-layouts, local(): block_out.astype(jnp.float32)  7 us
    gather x1, local copies, waits for them, and re-layouts, local(): jnp.take(pieces, source_tile, axis=2)  5.85 us
  transfers between devices with their start and end apart: 1, of which 1 were waited for; matrix products, arithmetic and copies ran while one was open for 1% of the time, Pallas kernels for 0%

profile of v1, /device:TPU:0, one launch (start us, length us, event | category | flops | bytes accessed | tf_op | source)
XLA Modules:
  0.0 260.2 jit_solution(15730117516689083790)
XLA Ops:
  2.4 2.0 fusion.48
  5.5 1.2 fusion.55
  6.7 1.3 compare_and_fusion
  8.0 2.2 fusion.11
  11.0 1.4 reduce_sum.116
  17.1 1.7 fusion.9
  19.1 1.3 fusion.60
  20.3 1.2 fusion.62
  24.0 5.2 %maximum_maximum_fusion = bf16[3,4,96,8,256]{4,3,2,1,0:T(8,128)(2,1)} fusion(bf16[1,1,96,8,256]{4,3,2,1,0:T(8,128)(2,1)} %bitcast.139, bf16[1,1,96,8,256]{4,3,2,1,0:T(8,128)(2,1)} %bitcast.140, bf16[1,1,96,8,256]{4,3,2,1,0:T(8,128)(2,1)} %bitcast.141, bf16[1,1,96,8,256]{4,3,2,1,0:T(8,128)(2,1)} %bitcast.138, bf16[1,1,96,8,256]{4,3,2,1,0:T(8,128)(2,1)} %bitcast.143, ...), kind=kLoop, calls=%fused_computation.21 | loop fusion | flops 25952256 | bytes 9437184 | tf_op jit(solution)/shard_map/stack | solution.py:98
  29.2 5.9 %gather_fusion = bf16[96,3,4,8,256]{4,3,2,1,0:T(8,128)(2,1)} fusion(bf16[3,4,96,8,256]{4,3,2,1,0:T(8,128)(2,1)} %maximum_maximum_fusion, s32[1024]{0:T(1024)S(1)} %pad_clamp_fusion.1), kind=kCustom, calls=%fused_computation | custom fusion | bytes 9437568 | tf_op jit(solution)/shard_map/jit(_take)/gather | solution.py:100
  35.1 3.0 %select_bitcast_fusion = bf16[3,4,96,8,256]{4,3,1,0,2:T(8,128)(2,1)S(1)} fusion(bf16[96,3,4,8,256]{4,3,2,1,0:T(8,128)(2,1)} %gather_fusion, pred[96]{0:T(512)(128)(4,1)S(1)} %broadcast_compare_fusion, pred[96]{0:T(512)(128)(4,1)S(1)} %copy-done.5), kind=kLoop, calls=%fused_computation.22 | loop fusion | flops 4718592 | bytes 9437376 | tf_op jit(solution)/shard_map/jit(_where)/select_n | solution.py:99
  50.0 7.6 %all-to-all-start = ((bf16[16,3,4,6,8,256]{5,4,2,1,3,0:T(8,128)(2,1)}), bf16[16,3,4,6,8,256]{5,4,2,1,3,0:T(8,128)(2,1)}, u32[]{:S(2)}, u32[]{:S(2)}) async-start(bf16[16,3,4,6,8,256]{5,4,2,1,3,0:T(8,128)(2,1)} %fusion.13), calls=%async_computation | async-start | bytes 9437184 | tf_op jit(solution)/shard_map/all_to_all | solution.py:103
  57.8 1.2 convert_multiply_fusion.2
  59.0 85.3 %all-to-all-done = bf16[16,3,4,6,8,256]{5,4,2,1,3,0:T(8,128)(2,1)} async-done(((bf16[16,3,4,6,8,256]{5,4,2,1,3,0:T(8,128)(2,1)}), bf16[16,3,4,6,8,256]{5,4,2,1,3,0:T(8,128)(2,1)}, u32[]{:S(2)}, u32[]{:S(2)}) %all-to-all-start) | async-done | bytes 4718624 | tf_op jit(solution)/shard_map/all_to_all | solution.py:103
  144.3 4.9 %copy.98 = bf16[3,4,96,8,256]{4,3,2,1,0:T(8,128)(2,1)} copy(bf16[3,4,96,8,256]{4,3,1,0,2:T(8,128)(2,1)} %bitcast.32) | data formatting | bytes 9437184 | tf_op jit(solution)/shard_map/reshape | solution.py:102
  149.2 4.2 %gather_fusion.1 = bf16[32,3,4,8,256]{4,3,2,1,0:T(8,128)(2,1)} fusion(bf16[3,4,96,8,256]{4,3,2,1,0:T(8,128)(2,1)} %copy.98, s32[1024]{0:T(1024)S(1)} %pad_clamp_fusion), kind=kCustom, calls=%fused_computation.1 | custom fusion | bytes 3145856 | tf_op jit(solution)/shard_map/jit(_take)/gather | solution.py:106
  153.5 1.6 select_bitcast_fusion.1
  158.2 2.7 %fusion.12 = bf16[512,256]{1,0:T(8,128)(2,1)} fusion(bf16[512,6912]{1,0:T(8,128)(2,1)S(1)} %constant_dynamic-update-slice_fusion, bf16[6912,256]{1,0:T(8,128)(2,1)S(1)} %bitcast.133, f32[256]{0:T(256)S(1)} %copy-done.7), kind=kOutput, calls=%fused_computation.40 | convolution fusion | flops 1812201472 | bytes 10880000 | tf_op jit(solution)/shard_map/dot_general | solution.py:41
  160.9 7.0 %reshape.414 = f32[2,32,8,32,8]{4,3,2,1,0:T(8,128)} reshape(bf16[512,256]{1,0:T(8,128)(2,1)} %fusion.12) | data formatting | bytes 786432 | tf_op jit(solution)/shard_map/convert_element_type | solution.py:109
  167.9 5.0 %fusion.58 = (f32[32,32]{1,0:T(8,128)S(1)}, f32[32,32]{1,0:T(8,128)S(1)}) fusion(f32[2,32,8,32,8]{4,3,2,1,0:T(8,128)} %reshape.414), kind=kLoop, calls=%fused_computation.186 | loop fusion | flops 391168 | bytes 532480 | tf_op jit(solution)/shard_map/reduce_sum | solution.py:112
  174.1 77.8 %all-reduce.2 = (f32[16,32]{1,0:T(8,128)}, f32[16,32]{1,0:T(8,128)}) all-reduce(f32[16,32]{1,0:T(8,128)S(1)} %fusion.30, f32[16,32]{1,0:T(8,128)S(1)} %fusion.32), channel_id=1, replica_groups=mesh['grp'=2,'tile'=16] {'tile'}, use_global_device_ids=true, to_apply=%region_14.15 | all-reduce | flops 1024 | bytes 8192 | tf_op jit(solution)/shard_map/psum | solution.py:115
  253.5 1.6 copy.127
  256.8 1.6 copy.129
  258.4 1.9 multiply_convert_fusion
  (118 shorter events, 29.1 us)
Async XLA Ops:
  0.6 157.4 %copy-start = (bf16[3,3,3,256,256]{4,3,2,1,0:T(8,128)(2,1)S(1)}, bf16[3,3,3,256,256]{4,3,2,1,0:T(8,128)(2,1)}, u32[]{:S(2)}) copy-start(bf16[3,3,3,256,256]{4,3,2,1,0:T(8,128)(2,1)} %param.14) | copy-start | bytes 10616836
  1.7 0.5 copy-start.4
  19.1 3.7 %copy-start.6 = (s32[96]{0:T(128)S(1)}, s32[96]{0:T(128)}, u32[]{:S(2)}) copy-start(s32[96]{0:T(128)} %fusion.55) | copy-start | bytes 1156
  29.2 5.9 %copy-start.5 = (pred[96]{0:T(512)(128)(4,1)S(1)}, pred[96]{0:T(512)(128)(4,1)}, u32[]{:S(2)}) copy-start(pred[96]{0:T(512)(128)(4,1)} %compare_and_fusion) | copy-start | bytes 292
  49.9 7.6 %copy-start.3 = (s32[16]{0:T(128)S(1)}, s32[16]{0:T(128)}, u32[]{:S(2)}) copy-start(s32[16]{0:T(128)} %get-tuple-element.11) | copy-start | bytes 196
  50.0 7.7 %copy-start.2 = (s32[16]{0:T(128)S(1)}, s32[16]{0:T(128)}, u32[]{:S(2)}) copy-start(s32[16]{0:T(128)} %param.11) | copy-start | bytes 196
  50.0 94.4 %all-to-all-start = ((bf16[16,3,4,6,8,256]{5,4,2,1,3,0:T(8,128)(2,1)}), bf16[16,3,4,6,8,256]{5,4,2,1,3,0:T(8,128)(2,1)}, u32[]{:S(2)}, u32[]{:S(2)}) async-start(bf16[16,3,4,6,8,256]{5,4,2,1,3,0:T(8,128)(2,1)} %fusion.13), calls=%async_computation | async-start | bytes 9437184 | tf_op jit(solution)/shard_map/all_to_all | solution.py:103
  57.7 115.2 %copy-start.1 = (s32[32]{0:T(128)}, s32[32]{0:T(128)S(1)}, u32[]{:S(2)}) copy-start(s32[32]{0:T(128)S(1)} %get-tuple-element.6) | copy-start | bytes 388
  157.5 0.7 copy-start.7
